TPU v7x, 512 devices: a whole 4x8x8 slice. The times are simulated.
512 devices in a mesh: frames: 64 (over x, y, core), tex: 8 (over z).
Axes of the slice: x: 4, y: 8, z: 8, core: 2. Of those that a mesh axis runs over, the one named last changes fastest.
Arguments:
- texture: bfloat16 [512, 16384], P('tex'), may hold values from -6 to 6
- requests: int32 [512, 32], P(('frames', 'tex')), may hold values from 0 to 63, as said below
- block_slot: int32 [512, 32], P(('frames', 'tex')), may hold values from 0 to 31
- texel_cell: int32 [512, 4096], P(('frames', 'tex')), may hold values from 0 to 960
- uv_frac: float32 [512, 2, 4096], P(('frames', 'tex')), may hold values from 0 to 1
- conv_weight: bfloat16 [32, 144], replicated, may hold values from -0.5 to 0.5
- cotangent: bfloat16 [512, 32, 4096], P(('frames', 'tex')), may hold values from -6 to 6
Outputs:
- rendered: bfloat16 [512, 32, 4096], P(('frames', 'tex'))
- texture_grad: float32 [512, 16384], P('tex', 'frames')
- weight_grad: float32 [32, 144], replicated
Inputs may be any that keep to these rules, and one draw needn't show every extreme that they name: The 4 tile numbers one renderer requests from one owner are distinct.
All inputs are finite; a program needn't handle non-finite values.
Results may differ from a plain program's by a relative error of at most 0.007.
Values may be sent and summed in bfloat16 or wider, within the bound.
No kernel may reach another device: no remote copies, remote signals or barrier semaphores. Data moves between devices by JAX's collectives and lax.ppermute only.
A program may use at most 64 MiB of HBM per device.

v0:
```python
import math
import jax
import jax.numpy as jnp
from jax import lax
from jax.sharding import PartitionSpec as P

CH = 16


def taps_and_weights(cell_row, frac_row, side):
    column = cell_row % (side - 1)
    row_index = cell_row // (side - 1)
    corner = row_index * side + column
    texel_taps = jnp.stack([corner, corner + 1, corner + side, corner + side + 1])
    frac_x = frac_row[0]
    frac_y = frac_row[1]
    weights = jnp.stack(
        [
            (1.0 - frac_x) * (1.0 - frac_y),
            frac_x * (1.0 - frac_y),
            (1.0 - frac_x) * frac_y,
            frac_x * frac_y,
        ]
    )
    return (texel_taps, weights)


def sample_matrix(texel_taps, weights, texel):
    positions = lax.broadcasted_iota(jnp.int32, (texel_taps.shape[1], texel), 1)
    matrix = jnp.zeros((texel_taps.shape[1], texel), jnp.float32)
    for number in range(4):
        matrix = matrix + jnp.where(
            texel_taps[number][:, None] == positions, weights[number][:, None], jnp.float32(0.0)
        )
    return matrix.astype(jnp.bfloat16)


def shifted(picture, shift_y, shift_x):
    height = picture.shape[1]
    width = picture.shape[2]
    padded_input = jnp.pad(picture, ((0, 0), (1, 1), (1, 1)))
    return padded_input[:, 1 + shift_y : 1 + shift_y + height, 1 + shift_x : 1 + shift_x + width]


def render_one(fetched, slot_row, cell_row, frac_row, conv_weight, cot_row):
    visible = fetched.shape[0]
    channels = fetched.shape[1]
    texel = fetched.shape[2]
    side = math.isqrt(texel)
    height = slot_row.shape[0]
    width = cell_row.shape[0] // height
    group_size = math.gcd(height, 16)
    group_count = height // group_size
    texel_taps, weights = taps_and_weights(cell_row, frac_row, side)
    taps_grouped = texel_taps.reshape(4, group_count, group_size * width).transpose(1, 0, 2)
    weights_grouped = weights.reshape(4, group_count, group_size * width).transpose(1, 0, 2)
    slots_grouped = slot_row.reshape(group_count, group_size)

    def forward(inputs):
        taps_part, weights_part, slots_part = inputs
        texture_lookup = sample_matrix(taps_part, weights_part, texel).reshape(
            group_size, width, texel
        )
        selected_entries = jnp.take(fetched, slots_part, axis=0)
        feature_maps = jnp.einsum(
            "qfm,qzm->qfz", selected_entries, texture_lookup, preferred_element_type=jnp.float32
        )
        return feature_maps.astype(jnp.bfloat16)

    grouped_features = lax.map(forward, (taps_grouped, weights_grouped, slots_grouped))
    feature_maps = grouped_features.transpose(2, 0, 1, 3).reshape(channels, height, width)
    offsets = [(shift_y, shift_x) for shift_y in (-1, 0, 1) for shift_x in (-1, 0, 1)]
    columns = jnp.concatenate(
        [shifted(feature_maps, shift_y, shift_x) for shift_y, shift_x in offsets], axis=0
    )
    columns = columns.reshape(9 * channels, height * width)
    preact = jnp.dot(conv_weight, columns, preferred_element_type=jnp.float32)
    sigmoid_pre = jax.nn.sigmoid(preact)
    rendered = (preact * sigmoid_pre).astype(jnp.bfloat16)
    pre_grad = (
        cot_row.astype(jnp.float32) * sigmoid_pre * (1.0 + preact * (1.0 - sigmoid_pre))
    ).astype(jnp.bfloat16)
    weight_local = jnp.einsum("op,kp->ok", pre_grad, columns, preferred_element_type=jnp.float32)
    col_grad = jnp.einsum("ok,op->kp", conv_weight, pre_grad, preferred_element_type=jnp.float32)
    col_grad = col_grad.reshape(9, channels, height, width)
    feat_grad = jnp.zeros((channels, height, width), jnp.float32)
    for number in range(9):
        shift_y, shift_x = offsets[number]
        feat_grad = feat_grad + shifted(col_grad[number], -shift_y, -shift_x)
    feat_grad = feat_grad.astype(jnp.bfloat16)
    grad_grouped = feat_grad.reshape(channels, group_count, group_size, width).transpose(1, 2, 0, 3)
    slot_numbers = jnp.arange(visible, dtype=jnp.int32)

    def backward(totals, inputs):
        taps_part, weights_part, slots_part, gradient_portion = inputs
        texture_lookup = sample_matrix(taps_part, weights_part, texel).reshape(
            group_size, width, texel
        )
        texel_gradient = jnp.einsum(
            "rzs,rsu->rzu", gradient_portion, texture_lookup, preferred_element_type=jnp.float32
        )
        selector = (slots_part[:, None] == slot_numbers[None, :]).astype(jnp.float32)
        added = jnp.einsum("gv,gct->vct", selector, texel_gradient, precision=lax.Precision.HIGHEST)
        return (totals + added, None)

    start = jnp.zeros((visible, channels, texel), jnp.float32)
    slot_grad, unused = lax.scan(
        backward, start, (taps_grouped, weights_grouped, slots_grouped, grad_grouped)
    )
    return (rendered, slot_grad.reshape(visible, channels * texel), weight_local)


def per_device(texture, requests, block_slot, texel_cell, uv_frac, conv_weight, cotangent):
    owners = lax.axis_size("tex")
    frame_count = lax.axis_size("frames")
    tile_count = texture.shape[0]
    tile_width = texture.shape[1]
    wanted_ids = requests.reshape(owners, -1)
    wanted = lax.all_to_all(wanted_ids, "tex", split_axis=0, concat_axis=0, tiled=True)
    served = jnp.take(texture, wanted.reshape(-1), axis=0).reshape(
        wanted.shape[0], wanted.shape[1], tile_width
    )
    returned_tiles = lax.all_to_all(served, "tex", split_axis=0, concat_axis=0, tiled=True)
    fetched = returned_tiles
    per_owner = fetched.shape[1]
    visible = owners * per_owner
    fetched = fetched.reshape(visible, CH, tile_width // CH)
    rendered, slot_grad, weight_local = render_one(
        fetched, block_slot[0], texel_cell[0], uv_frac[0], conv_weight, cotangent[0]
    )
    columns = tile_width // frame_count
    spread = slot_grad.reshape(visible, frame_count, columns).transpose(1, 0, 2)
    gathered = lax.all_to_all(spread, "frames", split_axis=0, concat_axis=0, tiled=True)
    gathered = gathered.reshape(frame_count, owners, per_owner, columns)
    senders = lax.all_gather(requests[0], "frames").reshape(frame_count, owners, per_owner)
    tile_numbers = jnp.arange(tile_count, dtype=jnp.int32)
    selector = (senders[None] == tile_numbers[:, None, None, None]).astype(jnp.float32)
    partial = jnp.einsum("qfoj,fojc->oqc", selector, gathered, precision=lax.Precision.HIGHEST)
    texture_grad = lax.psum_scatter(partial, "tex", scatter_dimension=0, tiled=True)
    texture_grad = texture_grad.reshape(tile_count, columns)
    norm_scale = 1.0 / math.sqrt(frame_count * owners * cotangent.shape[2])
    weight_grad = lax.psum(weight_local, ("frames", "tex")) * norm_scale
    return (rendered[None], texture_grad, weight_grad)


def solution(mesh):
    placed = (
        P("tex", None),
        P(("frames", "tex"), None),
        P(("frames", "tex"), None),
        P(("frames", "tex"), None),
        P(("frames", "tex"), None, None),
        P(),
        P(("frames", "tex"), None, None),
    )
    return jax.shard_map(
        per_device,
        mesh=mesh,
        in_specs=placed,
        out_specs=(P(("frames", "tex"), None, None), P("tex", "frames"), P()),
        check_vma=False,
    )
```

profile of v0, /device:TPU:1, one launch (start us, length us, event | category | flops | bytes accessed | tf_op | source)
XLA Modules:
  0.0 316.9 jit_solution(3174709285711801497)
XLA Ops:
  7.2 0.0 copy-start
  7.2 0.5 broadcast.244
  7.7 1.4 reduce.10
  9.1 0.7 all_to_all.12
  9.8 10.9 %all-to-all-start = ((s32[8,1,4]{2,1,0:T(1,128)}), s32[8,1,4]{2,1,0:T(1,128)S(1)}, u32[]{:S(2)}, u32[]{:S(2)}) async-start(s32[8,1,4]{2,1,0:T(1,128)} %bitcast.12), calls=%async_computation | async-start | bytes 8192 | tf_op jit(solution)/shard_map/all_to_all | solution.py:119
  20.7 0.9 fusion.38
  21.6 0.1 maximum_bitcast_fusion
  21.6 1.3 reduce.9
  23.0 0.1 reshape_squeeze.3
  23.1 4.1 %all-to-all-done = s32[8,1,4]{2,1,0:T(1,128)S(1)} async-done(((s32[8,1,4]{2,1,0:T(1,128)}), s32[8,1,4]{2,1,0:T(1,128)S(1)}, u32[]{:S(2)}, u32[]{:S(2)}) %all-to-all-start) | async-done | bytes 160 | tf_op jit(solution)/shard_map/all_to_all | solution.py:119
  27.1 0.7 reduce.11
  27.8 0.1 reshape.366
  27.9 1.2 gather_fusion.1
  29.1 1.2 gather.11
  30.3 0.1 copy.23
  30.4 0.1 copy.24
  30.5 2.7 broadcast_select_fusion
  33.3 3.6 %all-to-all-start.1 = ((bf16[8,4,16384]{2,1,0:T(4,128)(2,1)}), bf16[8,4,16384]{2,1,0:T(4,128)(2,1)S(1)}, u32[]{:S(2)}, u32[]{:S(2)}) async-start(bf16[8,4,16384]{2,1,0:T(4,128)(2,1)} %broadcast_select_fusion), calls=%async_computation.1 | async-start | bytes 2097152 | tf_op jit(solution)/shard_map/all_to_all | solution.py:123
  36.8 0.0 copy-done.4
  36.8 0.2 broadcast_add_fusion.2
  37.0 0.1 add_bitcast_fusion
  37.1 28.8 %all-to-all-done.1 = bf16[8,4,16384]{2,1,0:T(4,128)(2,1)S(1)} async-done(((bf16[8,4,16384]{2,1,0:T(4,128)(2,1)}), bf16[8,4,16384]{2,1,0:T(4,128)(2,1)S(1)}, u32[]{:S(2)}, u32[]{:S(2)}) %all-to-all-start.1) | async-done | bytes 1048608 | tf_op jit(solution)/shard_map/all_to_all | solution.py:123
  65.9 1.6 reshape.367
  67.5 16.0 %while.21 = (s32[]{:T(128)}, bf16[2,16,16,128]{3,2,1,0:T(8,128)(2,1)S(1)}, s32[2,16]{1,0:T(2,128)S(1)}, bf16[32,16,1024]{2,1,0:T(8,128)(2,1)}, s32[2,4,2048]{2,1...) while((s32[]{:T(128)}, ...), condition=%wide.region_1.2_spmd, body=%wide.region_0.1_spmd.sunk | while | flops 92570768 | bytes 1840141 | solution.py:70
  67.6 1.8 gather_fusion
  69.5 6.1 %fusion.57 = bf16[2,16,16,128]{3,2,1,0:T(8,128)(2,1)S(1)} fusion(bf16[2,16,16,128]{3,2,1,0:T(8,128)(2,1)S(1)} %get-tuple-element.284, s32[]{:T(128)} %get-tuple-element.283, f32[16,128]{1,0:T(8,128)S(1)} %bitcast.209, s32[16,128]{1,0:T(8,128)S(1)} %bitcast.213, f32[16,128]{1,0:T(8,128)S(1)} %bitcast.207, s32[16,128]{1,0:T(8,128)S(1)} %bitcast.211, ...), kind=kOutput, calls=%fused_computation.11.clone.1 | convolution fusion | flops 92569600 | bytes 655876 | tf_op jit(solution)/shard_map/while/body/eval_jaxpr/qfm,qzm->qfz/dot_general | solution.py:65
  75.7 1.8 gather_fusion
  77.5 6.1 %fusion.57 = bf16[2,16,16,128]{3,2,1,0:T(8,128)(2,1)S(1)} fusion(bf16[2,16,16,128]{3,2,1,0:T(8,128)(2,1)S(1)} %get-tuple-element.284, s32[]{:T(128)} %get-tuple-element.283, f32[16,128]{1,0:T(8,128)S(1)} %bitcast.209, s32[16,128]{1,0:T(8,128)S(1)} %bitcast.213, f32[16,128]{1,0:T(8,128)S(1)} %bitcast.207, s32[16,128]{1,0:T(8,128)S(1)} %bitcast.211, ...), kind=kOutput, calls=%fused_computation.11.clone.1 | convolution fusion | flops 92569600 | bytes 655876 | tf_op jit(solution)/shard_map/while/body/eval_jaxpr/qfm,qzm->qfz/dot_general | solution.py:65
  83.5 0.0 copy-start.6
  83.6 0.3 pad_slice_fusion
  84.4 0.1 copy-done.6
  84.5 1.1 fusion.23
  85.6 0.5 convolution_bitcast_fusion
  86.1 0.2 slice_bitcast_fusion.4
  86.4 0.1 copy.42
  86.4 0.1 copy.43
  86.5 0.1 copy.44
  86.5 0.1 copy.45
  86.6 0.1 copy.47
  86.7 0.1 copy.48
  86.7 0.1 copy.49
  86.8 0.1 copy.50
  86.8 0.1 copy.46
  86.9 0.5 fusion.33
  87.4 0.7 copy.28
  88.1 20.5 %while.22 = (s32[]{:T(128)}, f32[32,16,1024]{2,0,1:T(8,128)}, s32[2,16]{1,0:T(2,128)S(1)}, bf16[2,16,16,128]{3,2,1,0:T(8,128)(2,1)}, s32[2,4,2048]{2,1,0:T(4,128...) while((s32[]{:T(128)}, f32[32,16,1024]{2,0,1:T(8,128)}, ...), condition=%wide.region_3.4_spmd.clone, body=%wide.region_2.3_spmd.clone.sunk | while | flops 193987072 | bytes 6554495 | solution.py:107
  88.2 6.4 %fusion.61 = f32[16,16,1024]{2,1,0:T(8,128)S(1)} fusion(f32[16,128]{1,0:T(8,128)S(1)} %bitcast.217, s32[16,128]{1,0:T(8,128)S(1)} %bitcast.221, f32[16,128]{1,0:T(8,128)S(1)} %bitcast.215, s32[16,128]{1,0:T(8,128)S(1)} %bitcast.219, f32[16,128]{1,0:T(8,128)S(1)} %bitcast.216, s32[16,128]{1,0:T(8,128)S(1)} %bitcast.220, f32[16,128]{1,0:T(8,128)S(1)} %bitcast.214, ...), kind=kOutput, calls=%fused_computation.36.clone.1 | convolution fusion | flops 92274688 | bytes 1180160 | tf_op jit(solution)/shard_map/while/body/eval_jaxpr/rzs,rsu->rzu/dot_general | solution.py:99
  94.6 3.0 select_add_fusion.2
  97.6 6.4 %fusion.61 = f32[16,16,1024]{2,1,0:T(8,128)S(1)} fusion(f32[16,128]{1,0:T(8,128)S(1)} %bitcast.217, s32[16,128]{1,0:T(8,128)S(1)} %bitcast.221, f32[16,128]{1,0:T(8,128)S(1)} %bitcast.215, s32[16,128]{1,0:T(8,128)S(1)} %bitcast.219, f32[16,128]{1,0:T(8,128)S(1)} %bitcast.216, s32[16,128]{1,0:T(8,128)S(1)} %bitcast.220, f32[16,128]{1,0:T(8,128)S(1)} %bitcast.214, ...), kind=kOutput, calls=%fused_computation.36.clone.1 | convolution fusion | flops 92274688 | bytes 1180160 | tf_op jit(solution)/shard_map/while/body/eval_jaxpr/rzs,rsu->rzu/dot_general | solution.py:99
  104.0 4.5 %select_add_fusion.2 = f32[32,16,1024]{2,0,1:T(8,128)} fusion(f32[32,16,1024]{2,0,1:T(8,128)} %get-tuple-element.317, f32[16,16,1024]{2,1,0:T(8,128)S(1)} %fusion.61, pred[]{:T(512)S(6)} %compare.12, s32[16]{0:T(128)S(1)} %fusion.62), kind=kOutput, calls=%fused_computation.37.clone.1 | convolution fusion | flops 101712384 | bytes 5242945 | tf_op jit(solution)/shard_map/while/body/eval_jaxpr/gv,gct->vct/dot_general | solution.py:103
  108.6 4.1 %copy.29 = f32[32,16,1024]{2,1,0:T(8,128)} copy(f32[32,16,1024]{2,0,1:T(8,128)} %get-tuple-element.73) | data formatting | bytes 4194304 | tf_op jit(solution)/shard_map/while | solution.py:107
  112.7 2.9 reshape_reshape.3
  115.6 4.1 %copy.30 = f32[64,32,256]{2,1,0:T(8,128)} copy(f32[64,32,256]{2,0,1:T(8,128)} %bitcast.186) | data formatting | bytes 4194304 | tf_op jit(solution)/shard_map/transpose | solution.py:132
  119.7 11.1 %all-to-all-start.2 = ((f32[64,32,256]{2,1,0:T(8,128)}), f32[64,32,256]{2,1,0:T(8,128)}, u32[]{:S(2)}, u32[]{:S(2)}) async-start(f32[64,32,256]{2,1,0:T(8,128)} %copy.30), calls=%async_computation.2 | async-start | bytes 4194304 | tf_op jit(solution)/shard_map/all_to_all | solution.py:133
  130.8 0.0 reduce-scatter.2.cloned.1.call-start
  130.9 77.5 %all-gather = s32[64,1,32]{2,1,0:T(1,128)S(1)} all-gather(s32[1,1,32]{2,1,0:T(1,128)S(1)} %bitcast.230), channel_id=1, replica_groups=mesh['frames'=64,'tex'=8] {'frames'}, dimensions={0}, use_global_device_ids=true | all-gather | bytes 8320 | tf_op jit(solution)/shard_map/all_gather | solution.py:135
  208.3 0.1 copy.27
  208.4 0.0 all-to-all-done.2
  208.4 2.8 copy.31
  211.2 1.9 convolution_bitcast_fusion.2
  213.1 0.0 reduce-scatter.2.cloned.1.call-update
  213.2 1.1 fusion.39
  214.3 95.1 %psum.7 = f32[32,144]{1,0:T(8,128)S(1)} all-reduce(f32[32,144]{1,0:T(8,128)} %fusion.39), channel_id=1, replica_groups=mesh['frames'=64,'tex'=8] {'frames','tex'}, use_global_device_ids=true, to_apply=%region_5.6 | all-reduce | flops 4608 | bytes 36864 | tf_op jit(solution)/shard_map/psum | solution.py:142
  309.4 0.6 broadcast_multiply_fusion
  (45 shorter events, 1.0 us)
Async XLA Ops:
  7.2 20.7 %copy-start = (bf16[64,16384]{1,0:T(8,128)(2,1)S(1)}, bf16[64,16384]{1,0:T(8,128)(2,1)}, u32[]{:S(2)}) copy-start(bf16[64,16384]{1,0:T(8,128)(2,1)} %param.11) | copy-start | bytes 6291460
  9.8 17.3 %all-to-all-start = ((s32[8,1,4]{2,1,0:T(1,128)}), s32[8,1,4]{2,1,0:T(1,128)S(1)}, u32[]{:S(2)}, u32[]{:S(2)}) async-start(s32[8,1,4]{2,1,0:T(1,128)} %bitcast.12), calls=%async_computation | async-start | bytes 8192 | tf_op jit(solution)/shard_map/all_to_all | solution.py:119
  30.5 6.3 %copy-start.4 = (s32[1,4096]{1,0:T(1,128)S(1)}, s32[1,4096]{1,0:T(1,128)}, u32[]{:S(2)}) copy-start(s32[1,4096]{1,0:T(1,128)} %param.14) | copy-start | bytes 49156
  33.3 32.7 %all-to-all-start.1 = ((bf16[8,4,16384]{2,1,0:T(4,128)(2,1)}), bf16[8,4,16384]{2,1,0:T(4,128)(2,1)S(1)}, u32[]{:S(2)}, u32[]{:S(2)}) async-start(bf16[8,4,16384]{2,1,0:T(4,128)(2,1)} %broadcast_select_fusion), calls=%async_computation.1 | async-start | bytes 2097152 | tf_op jit(solution)/shard_map/all_to_all | solution.py:123
  83.5 0.9 copy-start.3
  83.5 1.0 copy-start.6
  84.5 1.1 copy-start.1
  119.7 11.2 %copy-start.5 = (s32[1,32]{1,0:T(1,128)S(1)}, s32[1,32]{1,0:T(1,128)}, u32[]{:S(2)}) copy-start(s32[1,32]{1,0:T(1,128)} %param.12) | copy-start | bytes 388
  119.7 88.7 %all-to-all-start.2 = ((f32[64,32,256]{2,1,0:T(8,128)}), f32[64,32,256]{2,1,0:T(8,128)}, u32[]{:S(2)}, u32[]{:S(2)}) async-start(f32[64,32,256]{2,1,0:T(8,128)} %copy.30), calls=%async_computation.2 | async-start | bytes 4194304 | tf_op jit(solution)/shard_map/all_to_all | solution.py:133
  130.8 179.2 %reduce-scatter.2.cloned.1.call-start = ((), (), s32[]{:S(2)}) async-start(), calls=%async_computation.4 | async-start | bytes 589824 | tf_op jit(solution)/shard_map/reduce_scatter | solution.py:139
  211.2 1.9 copy-start.2
Sparse Core Ops, SparseCore 0:
  213.3 29.5 reduce-scatter.1
where the time goes:
time: 318 us; the launch traced here: 317 us
  blocking collectives  173 us (54%)
  matrix products  37 us (12%)
  waiting for transfers between devices  32.9 us (10%)
  local copies, waits for them, and re-layouts  26.6 us (8%)
  starting transfers between devices  25.6 us (8%)
  between operations  14.4 us (5%)
  other arithmetic  7.69 us (2%)
    psum x1, blocking collectives, per_device(): weight_grad = lax.psum(weight_local, ('frames', 'tex')) * norm_scale  95.1 us
    all_gather x1, blocking collectives, per_device(): lax.all_gather(requests[0], 'frames')  77.5 us
    all_to_all x1, waiting for transfers between devices, per_device(): lax.all_to_all(served, 'tex', split_axis=0, concat_axis=0, tiled=True)  28.8 us
    dot_general x2, matrix products, backward(): jnp.einsum('rzs,rsu->rzu', gradient_portion, texture_lookup, preferred_el...  12.8 us
    dot_general x2, matrix products, forward(): jnp.einsum('qfm,qzm->qfz', selected_entries, texture_lookup, preferred_el...  12.1 us
    all_to_all x1, starting transfers between devices, per_device(): lax.all_to_all(spread, 'frames', split_axis=0, concat_axis=0, tiled=True)  11.1 us
    all_to_all x1, starting transfers between devices, per_device(): lax.all_to_all(wanted_ids, 'tex', split_axis=0, concat_axis=0, tiled=True)  10.9 us
    dot_general x2, matrix products, backward(): jnp.einsum('gv,gct->vct', selector, texel_gradient, precision=lax.Precisi...  7.51 us
  transfers between devices with their start and end apart: 4, of which 2 were waited for; matrix products, arithmetic and copies ran while one was open for 1% of the time, Pallas kernels for 0%

commit v1 on v0

--- a/solution.py
+++ b/solution.py
@@ -139,7 +139,7 @@
     texture_grad = lax.psum_scatter(partial, "tex", scatter_dimension=0, tiled=True)
     texture_grad = texture_grad.reshape(tile_count, columns)
     norm_scale = 1.0 / math.sqrt(frame_count * owners * cotangent.shape[2])
-    weight_grad = lax.psum(weight_local, ("frames", "tex")) * norm_scale
+    weight_grad = jnp.sum(lax.all_gather(weight_local, ("frames", "tex")), axis=0) * norm_scale
     return (rendered[None], texture_grad, weight_grad)
 
 

time: 318 us -> 262 us (0.82); the launches traced: 317 us -> 257 us
  blocking collectives: 173 us -> 82.2 us
  waiting for transfers between devices: 32.9 us -> 55.1 us
  other arithmetic: 7.69 us -> 14.5 us
    psum x1 -> x0, blocking collectives: 95.1 us -> none  [per_device(): weight_grad = lax.psum(weight_local, ('frames', 'tex')) * norm_scale]
    reduce_scatter x1, waiting for transfers between devices: 0.01 us -> 21.2 us  [per_device(): lax.psum_scatter(partial, 'tex', scatter_dimension=0, tiled=True)]
    reduce_sum x0 -> x1, other arithmetic: none -> 6.74 us  [per_device(): jnp.sum(lax.all_gather(weight_local, ('frames', 'tex')), axis=0)]
    all_gather x1, blocking collectives: 77.5 us -> 82.2 us  [per_device(): lax.all_gather(requests[0], 'frames')]
  transfers between devices with their start and end apart: 4 -> 5, of which waited for: 2 -> 4; matrix products, arithmetic and copies ran while one was open for 1% -> 19% of each run, Pallas kernels for 0% -> 0%
where the time goes in v1:
time: 262 us; the launch traced here: 257 us
  blocking collectives  82.2 us (31%)
  waiting for transfers between devices  55.1 us (21%)
  matrix products  38.7 us (15%)
  starting transfers between devices  25.6 us (10%)
  local copies, waits for them, and re-layouts  25.2 us (10%)
  between operations  15.8 us (6%)
  other arithmetic  14.5 us (6%)
    all_gather x1, blocking collectives, per_device(): lax.all_gather(requests[0], 'frames')  82.2 us
    all_to_all x1, waiting for transfers between devices, per_device(): lax.all_to_all(served, 'tex', split_axis=0, concat_axis=0, tiled=True)  28 us
    reduce_scatter x1, waiting for transfers between devices, per_device(): lax.psum_scatter(partial, 'tex', scatter_dimension=0, tiled=True)  21.2 us
    dot_general x2, matrix products, backward(): jnp.einsum('rzs,rsu->rzu', gradient_portion, texture_lookup, preferred_el...  14.5 us
    dot_general x2, matrix products, forward(): jnp.einsum('qfm,qzm->qfz', selected_entries, texture_lookup, preferred_el...  12.1 us
    all_to_all x1, starting transfers between devices, per_device(): lax.all_to_all(spread, 'frames', split_axis=0, concat_axis=0, tiled=True)  11.1 us
    all_to_all x1, starting transfers between devices, per_device(): lax.all_to_all(wanted_ids, 'tex', split_axis=0, concat_axis=0, tiled=True)  10.9 us
    dot_general x2, matrix products, backward(): jnp.einsum('gv,gct->vct', selector, texel_gradient, precision=lax.Precisi...  7.5 us
  transfers between devices with their start and end apart: 5, of which 4 were waited for; matrix products, arithmetic and copies ran while one was open for 19% of the time, Pallas kernels for 0%

profile of v1, /device:TPU:1, one launch (start us, length us, event | category | flops | bytes accessed | tf_op | source)
XLA Modules:
  0.0 257.3 jit_solution(11330770489928704566)
XLA Ops:
  8.0 0.0 copy-start
  8.0 0.5 broadcast.244
  8.5 1.4 reduce.10
  10.0 0.7 all_to_all.12
  10.6 10.9 %all-to-all-start = ((s32[8,1,4]{2,1,0:T(1,128)}), s32[8,1,4]{2,1,0:T(1,128)S(1)}, u32[]{:S(2)}, u32[]{:S(2)}) async-start(s32[8,1,4]{2,1,0:T(1,128)} %bitcast.12), calls=%async_computation | async-start | bytes 8192 | tf_op jit(solution)/shard_map/all_to_all | solution.py:119
  21.5 0.9 broadcast_add_fusion.2
  22.4 5.6 %all-to-all-done = s32[8,1,4]{2,1,0:T(1,128)S(1)} async-done(((s32[8,1,4]{2,1,0:T(1,128)}), s32[8,1,4]{2,1,0:T(1,128)S(1)}, u32[]{:S(2)}, u32[]{:S(2)}) %all-to-all-start) | async-done | bytes 160 | tf_op jit(solution)/shard_map/all_to_all | solution.py:119
  28.0 0.7 reduce.11
  28.6 0.1 reshape.366
  28.7 1.2 gather_fusion.1
  30.0 1.2 gather.11
  31.2 0.1 copy.23
  31.3 0.1 copy.24
  31.4 2.7 %broadcast_select_fusion = bf16[8,4,16384]{2,1,0:T(4,128)(2,1)} fusion(bf16[8,4,16384]{2,1,0:T(4,128)(2,1)} %gather.11, pred[8,4]{1,0:T(8,128)(4,1)S(1)} %copy.24), kind=kLoop, calls=%fused_computation.60 | loop fusion | flops 524288 | bytes 2097184 | tf_op jit(solution)/shard_map/jit(_take)/select_n | solution.py:120
  34.1 3.6 %all-to-all-start.1 = ((bf16[8,4,16384]{2,1,0:T(4,128)(2,1)}), bf16[8,4,16384]{2,1,0:T(4,128)(2,1)S(1)}, u32[]{:S(2)}, u32[]{:S(2)}) async-start(bf16[8,4,16384]{2,1,0:T(4,128)(2,1)} %broadcast_select_fusion), calls=%async_computation.1 | async-start | bytes 2097152 | tf_op jit(solution)/shard_map/all_to_all | solution.py:123
  37.7 0.0 all-gather.4.cloned.1.call-start
  37.8 0.7 reduce.9
  38.4 0.1 reshape_squeeze.3
  38.5 0.1 add_bitcast_fusion
  38.7 0.1 maximum_bitcast_fusion
  38.8 28.0 %all-to-all-done.1 = bf16[8,4,16384]{2,1,0:T(4,128)(2,1)S(1)} async-done(((bf16[8,4,16384]{2,1,0:T(4,128)(2,1)}), bf16[8,4,16384]{2,1,0:T(4,128)(2,1)S(1)}, u32[]{:S(2)}, u32[]{:S(2)}) %all-to-all-start.1) | async-done | bytes 1048608 | tf_op jit(solution)/shard_map/all_to_all | solution.py:123
  66.8 1.6 reshape.367
  68.4 16.0 %while.21 = (s32[]{:T(128)}, bf16[2,16,16,128]{3,2,1,0:T(8,128)(2,1)S(1)}, s32[2,16]{1,0:T(2,128)S(1)}, bf16[32,16,1024]{2,1,0:T(8,128)(2,1)}, s32[2,4,2048]{2,1...) while((s32[]{:T(128)}, ...), condition=%wide.region_1.2_spmd, body=%wide.region_0.1_spmd.sunk | while | flops 92570768 | bytes 1840149 | solution.py:70
  68.5 1.8 gather_fusion
  70.3 6.1 %fusion.57 = bf16[2,16,16,128]{3,2,1,0:T(8,128)(2,1)S(1)} fusion(bf16[2,16,16,128]{3,2,1,0:T(8,128)(2,1)S(1)} %get-tuple-element.284, s32[]{:T(128)S(6)} %copy.67, f32[16,128]{1,0:T(8,128)S(1)} %bitcast.211, s32[16,128]{1,0:T(8,128)S(1)} %bitcast.215, f32[16,128]{1,0:T(8,128)S(1)} %bitcast.209, s32[16,128]{1,0:T(8,128)S(1)} %bitcast.213, ...), kind=kOutput, calls=%fused_computation.11.clone.1 | convolution fusion | flops 92569600 | bytes 655876 | tf_op jit(solution)/shard_map/while/body/eval_jaxpr/qfm,qzm->qfz/dot_general | solution.py:65
  76.5 1.8 gather_fusion
  78.3 6.1 %fusion.57 = bf16[2,16,16,128]{3,2,1,0:T(8,128)(2,1)S(1)} fusion(bf16[2,16,16,128]{3,2,1,0:T(8,128)(2,1)S(1)} %get-tuple-element.284, s32[]{:T(128)S(6)} %copy.67, f32[16,128]{1,0:T(8,128)S(1)} %bitcast.211, s32[16,128]{1,0:T(8,128)S(1)} %bitcast.215, f32[16,128]{1,0:T(8,128)S(1)} %bitcast.209, s32[16,128]{1,0:T(8,128)S(1)} %bitcast.213, ...), kind=kOutput, calls=%fused_computation.11.clone.1 | convolution fusion | flops 92569600 | bytes 655876 | tf_op jit(solution)/shard_map/while/body/eval_jaxpr/qfm,qzm->qfz/dot_general | solution.py:65
  84.4 0.3 pad_slice_fusion
  85.3 0.1 copy-done.4
  85.4 1.1 fusion.23
  86.5 1.1 fusion.39
  87.6 0.0 all-gather.4.cloned.1.call-update
  87.6 0.5 convolution_bitcast_fusion
  88.1 0.2 slice_bitcast_fusion.4
  88.3 0.1 copy.42
  88.4 0.1 copy.43
  88.5 0.1 copy.44
  88.5 0.1 copy.45
  88.6 0.1 copy.47
  88.6 0.1 copy.48
  88.7 0.1 copy.49
  88.8 0.1 copy.50
  88.8 0.1 copy.46
  88.9 0.5 fusion.33
  89.4 0.1 copy.28
  89.4 22.2 %while.22 = (s32[]{:T(128)}, f32[32,16,1024]{2,0,1:T(8,128)}, s32[2,16]{1,0:T(2,128)S(1)}, bf16[2,16,16,128]{3,2,1,0:T(8,128)(2,1)S(1)}, s32[2,4,2048]{2,1,0:T(4...) while((s32[]{:T(128)}, f32[32,16,1024]{2,0,1:T(8,128)}, ...), condition=%wide.region_3.4_spmd.clone, body=%wide.region_2.3_spmd.clone.sunk | while | flops 193987072 | bytes 6553995 | solution.py:107
  89.5 7.3 %fusion.61 = f32[16,16,1024]{2,1,0:T(8,128)S(1)} fusion(f32[16,128]{1,0:T(8,128)S(1)} %bitcast.219, s32[16,128]{1,0:T(8,128)S(1)} %bitcast.223, f32[16,128]{1,0:T(8,128)S(1)} %bitcast.217, s32[16,128]{1,0:T(8,128)S(1)} %bitcast.221, f32[16,128]{1,0:T(8,128)S(1)} %bitcast.218, s32[16,128]{1,0:T(8,128)S(1)} %bitcast.222, f32[16,128]{1,0:T(8,128)S(1)} %bitcast.216, ...), kind=kOutput, calls=%fused_computation.36.clone.1 | convolution fusion | flops 92274688 | bytes 1179652 | tf_op jit(solution)/shard_map/while/body/eval_jaxpr/rzs,rsu->rzu/dot_general | solution.py:99
  96.8 3.0 %select_add_fusion.2 = f32[32,16,1024]{2,0,1:T(8,128)} fusion(f32[32,16,1024]{2,0,1:T(8,128)} %get-tuple-element.317, f32[16,16,1024]{2,1,0:T(8,128)S(1)} %fusion.61, pred[]{:T(512)S(6)} %compare.12, s32[16]{0:T(128)S(1)} %fusion.62), kind=kOutput, calls=%fused_computation.37.clone.1 | convolution fusion | flops 101712384 | bytes 5242945 | tf_op jit(solution)/shard_map/while/body/eval_jaxpr/gv,gct->vct/dot_general | solution.py:103
  99.8 7.3 %fusion.61 = f32[16,16,1024]{2,1,0:T(8,128)S(1)} fusion(f32[16,128]{1,0:T(8,128)S(1)} %bitcast.219, s32[16,128]{1,0:T(8,128)S(1)} %bitcast.223, f32[16,128]{1,0:T(8,128)S(1)} %bitcast.217, s32[16,128]{1,0:T(8,128)S(1)} %bitcast.221, f32[16,128]{1,0:T(8,128)S(1)} %bitcast.218, s32[16,128]{1,0:T(8,128)S(1)} %bitcast.222, f32[16,128]{1,0:T(8,128)S(1)} %bitcast.216, ...), kind=kOutput, calls=%fused_computation.36.clone.1 | convolution fusion | flops 92274688 | bytes 1179652 | tf_op jit(solution)/shard_map/while/body/eval_jaxpr/rzs,rsu->rzu/dot_general | solution.py:99
  107.1 4.5 %select_add_fusion.2 = f32[32,16,1024]{2,0,1:T(8,128)} fusion(f32[32,16,1024]{2,0,1:T(8,128)} %get-tuple-element.317, f32[16,16,1024]{2,1,0:T(8,128)S(1)} %fusion.61, pred[]{:T(512)S(6)} %compare.12, s32[16]{0:T(128)S(1)} %fusion.62), kind=kOutput, calls=%fused_computation.37.clone.1 | convolution fusion | flops 101712384 | bytes 5242945 | tf_op jit(solution)/shard_map/while/body/eval_jaxpr/gv,gct->vct/dot_general | solution.py:103
  111.7 4.1 %copy.29 = f32[32,16,1024]{2,1,0:T(8,128)} copy(f32[32,16,1024]{2,0,1:T(8,128)} %get-tuple-element.73) | data formatting | bytes 4194304 | tf_op jit(solution)/shard_map/while | solution.py:107
  115.8 2.9 %reshape_reshape.3 = f32[32,64,256]{2,1,0:T(8,128)} reshape(f32[32,16,1024]{2,1,0:T(8,128)} %copy.29) | data formatting | bytes 4194304 | tf_op jit(solution)/shard_map/reshape;reshape | solution.py:132
  118.7 4.1 %copy.30 = f32[64,32,256]{2,1,0:T(8,128)} copy(f32[64,32,256]{2,0,1:T(8,128)} %bitcast.188) | data formatting | bytes 4194304 | tf_op jit(solution)/shard_map/transpose | solution.py:132
  122.8 11.1 %all-to-all-start.2 = ((f32[64,32,256]{2,1,0:T(8,128)}), f32[64,32,256]{2,1,0:T(8,128)}, u32[]{:S(2)}, u32[]{:S(2)}) async-start(f32[64,32,256]{2,1,0:T(8,128)} %copy.30), calls=%async_computation.2 | async-start | bytes 4194304 | tf_op jit(solution)/shard_map/all_to_all | solution.py:133
  133.9 0.0 reduce-scatter.2.cloned.1.call-start
  134.0 82.2 %all-gather.1 = s32[64,1,32]{2,1,0:T(1,128)S(1)} all-gather(s32[1,1,32]{2,1,0:T(1,128)S(1)} %bitcast.232), channel_id=1, replica_groups=mesh['frames'=64,'tex'=8] {'frames'}, dimensions={0}, use_global_device_ids=true | all-gather | bytes 8320 | tf_op jit(solution)/shard_map/all_gather | solution.py:135
  216.2 0.1 copy.27
  216.2 2.8 %copy.31 = f32[64,32,256]{2,0,1:T(8,128)S(1)} copy(f32[64,32,256]{2,1,0:T(8,128)} %all-to-all-done.2) | data formatting | bytes 4194304 | tf_op jit(solution)/shard_map/all_to_all | solution.py:133
  219.1 1.9 convolution_bitcast_fusion.2
  221.0 0.0 reduce-scatter.2.cloned.1.call-update
  221.0 0.3 all-gather.4.cloned.1.call-done
  221.3 6.7 %reduce_sum.9 = f32[32,144]{1,0:T(8,128)S(1)} reduce(f32[512,32,144]{2,1,0:T(8,128)} %bitcast.186, f32[]{:T(128)} %constant.93.clone.1), dimensions={0}, to_apply=%region_5.6 | reduce | flops 2354688 | bytes 9455620 | tf_op jit(solution)/shard_map/reduce_sum | solution.py:142
  228.0 0.6 broadcast_multiply_fusion
  228.7 21.2 %reduce-scatter.2.cloned.1.call-done = f32[1,64,256]{2,1,0:T(8,128)} async-done(((f32[8,64,256]{2,1,0:T(8,128)}), f32[1,64,256]{2,1,0:T(8,128)}) %reduce-scatter.2.cloned.1.call-update) | async-done | bytes 65552 | tf_op jit(solution)/shard_map/reduce_scatter | solution.py:139
  (46 shorter events, 1.0 us)
Async XLA Ops:
  8.0 20.7 %copy-start = (bf16[64,16384]{1,0:T(8,128)(2,1)S(1)}, bf16[64,16384]{1,0:T(8,128)(2,1)}, u32[]{:S(2)}) copy-start(bf16[64,16384]{1,0:T(8,128)(2,1)} %param.11) | copy-start | bytes 6291460
  10.6 17.3 %all-to-all-start = ((s32[8,1,4]{2,1,0:T(1,128)}), s32[8,1,4]{2,1,0:T(1,128)S(1)}, u32[]{:S(2)}, u32[]{:S(2)}) async-start(s32[8,1,4]{2,1,0:T(1,128)} %bitcast.12), calls=%async_computation | async-start | bytes 8192 | tf_op jit(solution)/shard_map/all_to_all | solution.py:119
  31.4 6.4 %copy-start.5 = (s32[1,32]{1,0:T(1,128)S(1)}, s32[1,32]{1,0:T(1,128)}, u32[]{:S(2)}) copy-start(s32[1,32]{1,0:T(1,128)} %param.13) | copy-start | bytes 388
  31.4 7.2 %copy-start.1 = (f32[1,2,4096]{2,1,0:T(2,128)S(1)}, f32[1,2,4096]{2,1,0:T(2,128)}, u32[]{:S(2)}) copy-start(f32[1,2,4096]{2,1,0:T(2,128)} %param.15) | copy-start | bytes 98308
  34.1 32.7 %all-to-all-start.1 = ((bf16[8,4,16384]{2,1,0:T(4,128)(2,1)}), bf16[8,4,16384]{2,1,0:T(4,128)(2,1)S(1)}, u32[]{:S(2)}, u32[]{:S(2)}) async-start(bf16[8,4,16384]{2,1,0:T(4,128)(2,1)} %broadcast_select_fusion), calls=%async_computation.1 | async-start | bytes 2097152 | tf_op jit(solution)/shard_map/all_to_all | solution.py:123
  37.7 183.6 %all-gather.4.cloned.1.call-start = ((), (), s32[]{:S(2)}) async-start(), calls=%async_computation.5 | async-start | bytes 16809984 | tf_op jit(solution)/shard_map/all_gather | solution.py:142
  84.4 0.9 copy-start.2
  84.4 1.0 copy-start.4
  122.8 11.2 %copy-start.3 = (s32[1,32]{1,0:T(1,128)S(1)}, s32[1,32]{1,0:T(1,128)}, u32[]{:S(2)}) copy-start(s32[1,32]{1,0:T(1,128)} %param.12) | copy-start | bytes 388
  122.8 93.4 %all-to-all-start.2 = ((f32[64,32,256]{2,1,0:T(8,128)}), f32[64,32,256]{2,1,0:T(8,128)}, u32[]{:S(2)}, u32[]{:S(2)}) async-start(f32[64,32,256]{2,1,0:T(8,128)} %copy.30), calls=%async_computation.2 | async-start | bytes 4194304 | tf_op jit(solution)/shard_map/all_to_all | solution.py:133
  133.9 115.9 %reduce-scatter.2.cloned.1.call-start = ((), (), s32[]{:S(2)}) async-start(), calls=%async_computation.4 | async-start | bytes 589824 | tf_op jit(solution)/shard_map/reduce_scatter | solution.py:139
Sparse Core Ops, SparseCore 0:
  87.7 133.5 all-gather.3
Sparse Core Ops, SparseCore 1:
  221.1 28.7 reduce-scatter.1
